TPU v7x, 256 devices: a whole 4x4x8 slice. The times are simulated.
256 devices in a mesh: seq: 16 (over x_hi, z), row: 4 (over x_lo, core), col: 4 (over y).
Axes of the slice: x: 4 (x_hi: 2, x_lo: 2; x = x_hi * 2 + x_lo), y: 4, z: 8, core: 2. Of those that a mesh axis runs over, the one named last changes fastest.
Arguments:
- tokens: bfloat16 [8192, 4096], P(('seq', 'col'), 'row'), may hold values from -11 to 11
- w_query: bfloat16 [4096, 4096], P('row', 'col'), as said below
- w_key: bfloat16 [4096, 1024], P('row', 'col'), as said below
- w_value: bfloat16 [4096, 1024], P('row', 'col'), may hold values from -0.09375 to 0.09375
- w_output: bfloat16 [4096, 4096], P('col', 'row'), may hold values from -0.09375 to 0.09375
Outputs:
- attended: bfloat16 [8192, 4096], P(('seq', 'col'), 'row')
Inputs may be any that keep to these rules, and one draw needn't show every extreme that they name: `w_query`: entries below 6 / sqrt(4096) in magnitude. `w_key`: entries below 8.4 / sqrt(4096) in magnitude.
All inputs are finite; a program needn't handle non-finite values.
Results may differ from a plain program's by a relative error of at most 0.025.
Values may be sent and summed in bfloat16 or wider, within the bound.
No kernel may reach another device: no remote copies, remote signals or barrier semaphores. Data moves between devices by JAX's collectives and lax.ppermute only.
A program may use at most 64 MiB of HBM per device.

v0:
```python
import jax
import jax.numpy as jnp
from jax import lax
from jax.sharding import PartitionSpec as P

HEADS = 32
KV_HEADS = 8
HEAD_DIM = 128


rope_base = 500000.0
masked_score = -1e30


def rotate(values, positions):
    half = HEAD_DIM // 2
    freqs = rope_base ** (-(jnp.arange(half, dtype=jnp.float32) * 2.0) / HEAD_DIM)
    angles = positions.astype(jnp.float32)[:, None] * freqs[None, :]
    cosine = jnp.concatenate([jnp.cos(angles), jnp.cos(angles)], axis=1)
    sine = jnp.concatenate([jnp.sin(angles), jnp.sin(angles)], axis=1)
    count = values.shape[0]
    heads = values.reshape(count, -1, HEAD_DIM)
    turned = jnp.concatenate([-heads[..., half:], heads[..., :half]], axis=-1)
    result = heads * cosine[:, None, :] + turned * sine[:, None, :]
    return result.reshape(count, -1)


def swap_pairs(value, flip):
    count = lax.axis_size("row")
    return lax.ppermute(value, "row", [(r, r ^ flip) for r in range(count)])


def shifted(value, axis, step):
    count = lax.axis_size(axis)
    return lax.ppermute(value, axis, [(i, (i + step) % count) for i in range(count)])


def pick(flag, first, second):
    return jnp.where(flag, first, second)


def on_device(tokens, w_query, w_key, w_value, w_output):
    shard_rows = tokens.shape[0]
    col_count = lax.axis_size("col")
    row_count = lax.axis_size("row")
    seq_count = lax.axis_size("seq")
    block_len = shard_rows * col_count
    key_len = block_len // 2
    seq_at = lax.axis_index("seq")
    row_at = lax.axis_index("row")
    core = row_at % 2
    chip = row_at // 2
    width_q = w_query.shape[1]
    width_kv = w_key.shape[1]
    local_kv = width_kv // HEAD_DIM
    assert row_count == 2 * local_kv
    q_width = width_q // row_count
    score_scale = HEAD_DIM ** (-0.5)

    col_at = lax.axis_index("col")
    pieces = [tokens] + [shifted(tokens, "col", step) for step in range(1, col_count)]
    order = (col_at - jnp.arange(col_count, dtype=jnp.int32)) % col_count
    block_tokens = jnp.take(jnp.stack(pieces), order, axis=0).reshape(block_len, -1)
    part_q = jnp.dot(block_tokens, w_query, preferred_element_type=jnp.float32)
    part_k = jnp.dot(block_tokens, w_key, preferred_element_type=jnp.float32)
    part_v = jnp.dot(block_tokens, w_value, preferred_element_type=jnp.float32)
    q_chunks = part_q.reshape(block_len, row_count, q_width).transpose(1, 0, 2)
    q_chunks = q_chunks.reshape(2, 2, block_len * q_width // HEAD_DIM, HEAD_DIM)

    def kv_chunks(part):
        split = part.reshape(2, key_len, local_kv, HEAD_DIM).transpose(2, 0, 1, 3)
        return split

    chunks = jnp.concatenate([q_chunks, kv_chunks(part_k), kv_chunks(part_v)], axis=2)
    keep_a = lax.dynamic_index_in_dim(chunks, core, axis=1, keepdims=False)
    send_a = lax.dynamic_index_in_dim(chunks, 1 - core, axis=1, keepdims=False)
    summed_a = keep_a + swap_pairs(send_a, 1)
    keep_b = lax.dynamic_index_in_dim(summed_a, chip, axis=0, keepdims=False)
    send_b = lax.dynamic_index_in_dim(summed_a, 1 - chip, axis=0, keepdims=False)
    mine = keep_b + swap_pairs(send_b.astype(jnp.bfloat16), 2).astype(jnp.float32)

    q_rows = block_len * q_width // HEAD_DIM
    q_mine = mine[:q_rows].reshape(block_len, q_width)
    k_mine = mine[q_rows : q_rows + key_len]
    v_mine = mine[q_rows + key_len :]

    block_start = seq_at * block_len
    q_pos = block_start + jnp.arange(block_len, dtype=jnp.int32)
    k_offset = core * key_len + jnp.arange(key_len, dtype=jnp.int32)
    query = rotate(q_mine, q_pos).astype(jnp.bfloat16)
    keys = rotate(k_mine, block_start + k_offset).astype(jnp.bfloat16)
    kv_own = jnp.concatenate([keys, v_mine.astype(jnp.bfloat16)], axis=1)

    query_other = swap_pairs(query, 1)
    q_all = jnp.concatenate([query, query_other], axis=1)
    q_heads = q_all.reshape(block_len, -1, HEAD_DIM).transpose(1, 0, 2)
    n_heads = q_heads.shape[0]

    def attend(state, kv_rows, allowed):
        peak, total, summed = state
        key_blk = kv_rows[:, :HEAD_DIM]
        value_blk = kv_rows[:, HEAD_DIM:]
        scores = (
            jnp.einsum("hqd,kd->hqk", q_heads, key_blk, preferred_element_type=jnp.float32)
            * score_scale
        )
        scores = jnp.where(allowed[None], scores, masked_score)
        new_peak = jnp.maximum(peak, jnp.max(scores, axis=-1))
        weights = jnp.exp(scores - new_peak[..., None])
        factor = jnp.exp(peak - new_peak)
        total = total * factor + jnp.sum(weights, axis=-1)
        summed = summed * factor[..., None] + jnp.einsum(
            "hqk,kd->hqd",
            weights.astype(jnp.bfloat16),
            value_blk,
            preferred_element_type=jnp.float32,
        )
        return (new_peak, total, summed)

    state = (
        jnp.full((n_heads, block_len), masked_score, jnp.float32),
        jnp.zeros((n_heads, block_len), jnp.float32),
        jnp.zeros((n_heads, block_len, HEAD_DIM), jnp.float32),
    )
    kv_all = lax.all_gather(kv_own, "seq", axis=0, tiled=False)
    own_pos = block_start + k_offset
    state = attend(state, kv_own, own_pos[None, :] <= q_pos[:, None])
    per_chunk = 4
    for first in range(0, seq_count, per_chunk):
        kv_chunk = kv_all[first : first + per_chunk].reshape(per_chunk * key_len, -1)
        blocks = first + jnp.arange(per_chunk, dtype=jnp.int32)
        chunk_pos = (blocks[:, None] * block_len + k_offset[None, :]).reshape(-1)
        state = attend(state, kv_chunk, (chunk_pos < block_start)[None, :])

    peak, total, summed = state
    own = n_heads // 2
    other_peak, other_total, other_summed = swap_pairs(
        (peak[own:], total[own:], summed[own:]), 1
    )
    peak_mine = jnp.maximum(peak[:own], other_peak)
    factor_a = jnp.exp(peak[:own] - peak_mine)
    factor_b = jnp.exp(other_peak - peak_mine)
    total_mine = total[:own] * factor_a + other_total * factor_b
    summed_mine = summed[:own] * factor_a[..., None] + other_summed * factor_b[..., None]
    heads_mine = (summed_mine / total_mine[..., None]).transpose(1, 0, 2)
    heads_mine = heads_mine.reshape(block_len, q_width).astype(jnp.bfloat16)

    heads_pair_other = swap_pairs(heads_mine, 1)
    heads_pair = jnp.stack(
        [pick(core == 0, heads_mine, heads_pair_other), pick(core == 0, heads_pair_other, heads_mine)]
    )
    heads_quad_other = swap_pairs(heads_pair, 2)
    heads_quad = jnp.concatenate(
        [pick(chip == 0, heads_pair, heads_quad_other), pick(chip == 0, heads_quad_other, heads_pair)]
    )
    w_out = w_output.reshape(row_count, q_width, w_output.shape[1])
    partial_out = jnp.einsum(
        "rtc,rco->to", heads_quad, w_out, preferred_element_type=jnp.float32
    ).astype(jnp.bfloat16)
    out_chunks = partial_out.reshape(col_count, shard_rows, -1)
    result = lax.dynamic_index_in_dim(out_chunks, col_at, 0, keepdims=False).astype(jnp.float32)
    for step in range(1, col_count):
        target = (col_at + step) % col_count
        sent = lax.dynamic_index_in_dim(out_chunks, target, 0, keepdims=False)
        result = result + shifted(sent, "col", step).astype(jnp.float32)
    return result.astype(jnp.bfloat16)


def solution(mesh):
    return jax.shard_map(
        on_device,
        mesh=mesh,
        in_specs=(
            P(("seq", "col"), "row"),
            P("row", "col"),
            P("row", "col"),
            P("row", "col"),
            P("col", "row"),
        ),
        out_specs=P(("seq", "col"), "row"),
        check_vma=False,
    )
```

profile of v0, /device:TPU:2, one launch (start us, length us, event | category | flops | bytes accessed | tf_op | source)
XLA Modules:
  0.0 235.7 jit_solution(5418174351075474167)
XLA Ops:
  6.5 1.6 collective-permute-start
  8.1 1.7 collective-permute-start.2
  9.8 2.0 collective-permute-start.1
  11.9 2.0 copy.53
  14.0 2.0 copy.54
  16.0 4.0 %copy.52 = bf16[1024,1024]{1,0:T(8,128)(2,1)} copy(bf16[1024,1024]{0,1:T(8,128)(2,1)} %bitcast.146) | data formatting | bytes 4194304 | tf_op jit(solution)/shard_map/dot_general | solution.py:64
  20.0 1.2 collective-permute-done.2
  21.2 1.7 collective-permute-done.1
  22.9 1.1 pad_maximum_fusion
  24.0 1.8 gather_fusion
  26.1 1.7 convolution_bitcast_fusion.1
  28.2 2.6 %convolution_bitcast_fusion = f32[4,512,256]{2,1,0:T(8,128)} fusion(bf16[512,1024,1]{1,0,2:T(8,128)(2,1)S(1)} %bitcast.156, bf16[4,256,1024]{2,1,0:T(8,128)(2,1)S(1)} %bitcast.147), kind=kOutput, calls=%fused_computation.33 | convolution fusion | flops 1073741824 | bytes 5242880 | tf_op jit(solution)/shard_map/dot_general | solution.py:64
  30.9 2.6 %reshape.416 = f32[2,2,1024,128]{3,2,1,0:T(8,128)} reshape(f32[4,512,256]{2,1,0:T(8,128)} %convolution_bitcast_fusion) | data formatting | bytes 4194304 | tf_op jit(solution)/shard_map/reshape | solution.py:68
  33.5 1.7 constant_dynamic-update-slice_fusion
  35.3 1.9 constant_dynamic-slice_fusion.1
  37.2 3.0 %copy.29 = f32[2,1,1536,128]{2,3,0,1:T(8,128)} copy(f32[2,1,1536,128]{3,2,1,0:T(8,128)} %get-tuple-element.18) | data formatting | bytes 3145728 | tf_op jit(solution)/shard_map/jit(dynamic_index_in_dim)/dynamic_slice | solution.py:76
  40.2 3.1 %copy.28 = f32[2,1,1536,128]{2,3,0,1:T(8,128)} copy(f32[2,1,1536,128]{3,2,1,0:T(8,128)} %get-tuple-element.17) | data formatting | bytes 3145728 | tf_op jit(solution)/shard_map/jit(dynamic_index_in_dim)/dynamic_slice | solution.py:75
  43.9 2.1 bitcast_add_fusion
  46.0 1.2 copy-done.2
  47.2 11.6 %collective-permute-start.4 = (bf16[1536,128]{0,1:T(8,128)(2,1)S(1)}, bf16[1536,128]{0,1:T(8,128)(2,1)S(1)}, u32[]{:S(2)}, u32[]{:S(2)}) collective-permute-start(bf16[1536,128]{0,1:T(8,128)(2,1)S(1)} %fusion.61), channel_id=1, source_target_pairs={{0,8},{4,12},{8,0},{12,4},{1,9},{5,13},{9,1},{13,5},{2,10},{6,14},... | collective-permute-start | bytes 1179656 | tf_op jit(solution)/shard_map/ppermute | solution.py:30
  59.1 10.3 %collective-permute-done.4 = bf16[1536,128]{0,1:T(8,128)(2,1)S(1)} collective-permute-done((bf16[1536,128]{0,1:T(8,128)(2,1)S(1)}, bf16[1536,128]{0,1:T(8,128)(2,1)S(1)}, u32[]{:S(2)}, u32[]{:S(2)}) %collective-permute-start.4) | collective-permute-done | bytes 393248 | tf_op jit(solution)/shard_map/ppermute | solution.py:30
  69.4 1.2 bitcast_add_fusion.1
  72.1 1.0 multiply_cosine_fusion
  73.1 1.0 pad_maximum_fusion.3
  74.2 0.8 slice.116
  75.0 1.2 copy.30
  76.2 0.9 reshape_reshape.5
  77.8 2.5 %maximum_multiply_fusion = f32[512,2,128]{2,1,0:T(2,128)} fusion(f32[512,2,64]{2,1,0:T(2,128)S(1)} %get-tuple-element.29, f32[512,2,64]{2,1,0:T(2,128)S(1)} %get-tuple-element.28, f32[512,128]{1,0:T(8,128)} %get-tuple-element.59), kind=kLoop, calls=%fused_computation.67 | loop fusion | flops 262144 | bytes 1310720 | tf_op jit(solution)/shard_map/mul | solution.py:24
  80.2 2.0 copy.32
  82.3 2.0 copy.33
  84.3 1.1 mul.200
  85.5 1.8 fusion.44
  89.2 1.1 pad_maximum_fusion.1
  90.2 1.0 copy.34
  91.3 1.3 copy.35
  92.6 2.7 %fusion.24 = (f32[4,512]{1,0:T(4,128)S(1)}, f32[4,512,256]{1,2,0:T(8,128)}) fusion(pred[512,256]{0,1:T(8,128)(4,1)S(1)} %broadcast_compare_fusion, bf16[256,128]{0,1:T(8,128)(2,1)} %copy-done.6, bf16[512,4,128]{2,0,1:T(8,128)(2,1)S(1)} %copy.35), kind=kOutput, calls=%fused_computation.32 | convolution fusion | flops 135788544 | bytes 2826240 | tf_op jit(solution)/shard_map/hqd,kd->hqk/dot_general | solution.py:104
  95.3 62.2 %all-gather.3.cloned.1.call-done = bf16[4096,256]{0,1:T(8,128)(2,1)} async-done(((bf16[256,256]{0,1:T(8,128)(2,1)}), bf16[4096,256]{0,1:T(8,128)(2,1)}) %all-gather.3.cloned.1.call-update) | async-done | bytes 2097168 | tf_op jit(solution)/shard_map/all_gather | solution.py:125
  157.5 2.3 fusion
  159.9 2.3 fusion.1
  162.2 2.3 fusion.2
  164.5 2.5 %fusion.3 = (f32[4,512]{1,0:T(4,128)S(1)}, f32[4,512,1024]{2,1,0:T(8,128)S(1)}) fusion(pred[1024]{0:T(1024)(128)(4,1)S(1)} %lt.138, bf16[4096,256]{0,1:T(8,128)(2,1)} %all-gather.3.cloned.1.call-done, bf16[512,4,128]{2,0,1:T(8,128)(2,1)S(1)} %copy.35), kind=kOutput, calls=%fused_computation.12 | convolution fusion | flops 543160320 | bytes 9184256 | tf_op jit(solution)/shard_map/hqd,kd->hqk/dot_general | solution.py:104
  167.5 2.1 fusion.8
  169.6 2.1 fusion.6
  171.7 2.1 fusion.4
  173.7 2.3 fusion.10
  176.0 3.1 %fusion.14 = f32[4,512,128]{1,2,0:T(8,128)S(1)} fusion(f32[4,512,1024]{2,1,0:T(8,128)S(1)} %get-tuple-element.45, f32[4,512]{1,0:T(4,128)S(1)} %get-tuple-element.14, pred[1024]{0:T(1024)(128)(4,1)S(1)} %copy-done.9, bf16[4096,256]{0,1:T(8,128)(2,1)} %all-gather.3.cloned.1.call-done), kind=kOutput, calls=%fused_computation.22 | convolution fusion | flops 545259520 | bytes 9708544 | tf_op jit(solution)/shard_map/hqk,kd->hqd/dot_general | solution.py:112
  179.1 3.1 %fusion.16 = f32[4,512,128]{1,2,0:T(8,128)S(1)} fusion(f32[4,512,1024]{2,1,0:T(8,128)S(1)} %get-tuple-element.47, f32[4,512]{1,0:T(4,128)S(1)} %get-tuple-element.15, pred[1024]{0:T(1024)(128)(4,1)S(1)} %copy-done.8, bf16[4096,256]{0,1:T(8,128)(2,1)} %all-gather.3.cloned.1.call-done), kind=kOutput, calls=%fused_computation.23 | convolution fusion | flops 545259520 | bytes 9708544 | tf_op jit(solution)/shard_map/hqk,kd->hqd/dot_general | solution.py:112
  182.2 3.1 %fusion.18 = f32[4,512,128]{1,2,0:T(8,128)S(1)} fusion(f32[4,512,1024]{2,1,0:T(8,128)S(1)} %get-tuple-element.49, f32[4,512]{1,0:T(4,128)S(1)} %get-tuple-element.16, pred[1024]{0:T(1024)(128)(4,1)S(1)} %lt.132, bf16[4096,256]{0,1:T(8,128)(2,1)} %all-gather.3.cloned.1.call-done), kind=kOutput, calls=%fused_computation.24 | convolution fusion | flops 545259520 | bytes 9708544 | tf_op jit(solution)/shard_map/hqk,kd->hqd/dot_general | solution.py:112
  185.3 3.1 %fusion.12 = f32[4,512,128]{1,2,0:T(8,128)S(1)} fusion(f32[4,512,1024]{2,1,0:T(8,128)S(1)} %get-tuple-element.43, f32[4,512]{1,0:T(4,128)S(1)} %get-tuple-element.13, pred[1024]{0:T(1024)(128)(4,1)S(1)} %lt.138, bf16[4096,256]{0,1:T(8,128)(2,1)} %all-gather.3.cloned.1.call-done), kind=kOutput, calls=%fused_computation.21 | convolution fusion | flops 545259520 | bytes 9708544 | tf_op jit(solution)/shard_map/hqk,kd->hqd/dot_general | solution.py:112
  188.3 1.0 fusion.34
  190.2 1.2 collective-permute-done.8
  191.9 1.4 collective-permute-done.9
  193.3 0.8 pad_maximum_fusion.2
  194.2 1.7 collective-permute-start.10
  195.9 12.7 %collective-permute-done.10 = bf16[2,512,256]{2,1,0:T(8,128)(2,1)S(1)} collective-permute-done((bf16[2,512,256]{2,1,0:T(8,128)(2,1)}, bf16[2,512,256]{2,1,0:T(8,128)(2,1)S(1)}, u32[]{:S(2)}, u32[]{:S(2)}) %collective-permute-start.10) | collective-permute-done | bytes 524320 | tf_op jit(solution)/shard_map/ppermute | solution.py:30
  208.7 1.3 bitcast_convert_fusion
  210.0 0.8 dynamic-slice_bitcast_fusion.2
  210.8 1.5 collective-permute-start.11
  212.3 1.8 collective-permute-start.13
  214.0 1.8 collective-permute-start.12
  215.8 4.7 %collective-permute-done.11 = bf16[128,1024]{1,0:T(8,128)(2,1)} collective-permute-done((bf16[128,1024]{1,0:T(8,128)(2,1)}, bf16[128,1024]{1,0:T(8,128)(2,1)}, u32[]{:S(2)}, u32[]{:S(2)}) %collective-permute-start.11) | collective-permute-done | bytes 262176 | tf_op jit(solution)/shard_map/ppermute | solution.py:35
  220.5 4.2 %collective-permute-done.13 = bf16[128,1024]{1,0:T(8,128)(2,1)} collective-permute-done((bf16[128,1024]{1,0:T(8,128)(2,1)}, bf16[128,1024]{1,0:T(8,128)(2,1)}, u32[]{:S(2)}, u32[]{:S(2)}) %collective-permute-start.13) | collective-permute-done | bytes 262176 | tf_op jit(solution)/shard_map/ppermute | solution.py:35
  224.7 1.7 collective-permute-done.12
  226.4 2.0 fusion.49
  (74 shorter events, 7.9 us)
Async XLA Ops:
  6.5 202.1 %copy-start = (bf16[1024,1024]{1,0:T(8,128)(2,1)S(1)}, bf16[1024,1024]{1,0:T(8,128)(2,1)}, u32[]{:S(2)}) copy-start(bf16[1024,1024]{1,0:T(8,128)(2,1)} %param.9) | copy-start | bytes 6291460
  6.5 16.3 %copy-start.7 = (bf16[128,1024]{1,0:T(8,128)(2,1)S(1)}, bf16[128,1024]{1,0:T(8,128)(2,1)}, u32[]{:S(2)}) copy-start(bf16[128,1024]{1,0:T(8,128)(2,1)} %param.5) | copy-start | bytes 786436
  6.5 151.0 %all-gather.3.cloned.1.call-start = ((), (), s32[]{:S(2)}) async-start(), calls=%async_computation | async-start | bytes 2228224 | tf_op jit(solution)/shard_map/all_gather | solution.py:125
  6.5 13.5 %collective-permute-start = (bf16[128,1024]{1,0:T(8,128)(2,1)}, bf16[128,1024]{1,0:T(8,128)(2,1)S(1)}, u32[]{:S(2)}, u32[]{:S(2)}) collective-permute-start(bf16[128,1024]{1,0:T(8,128)(2,1)} %param.5), channel_id=1, source_target_pairs={{0,1},{1,2},{2,3},{3,0},{4,5},{5,6},{6,7},{7,4},{8,9},{9,10},{10,1... | collective-permute-start | bytes 786440 | tf_op jit(solution)/shard_map/ppermute | solution.py:35
  8.1 13.1 %collective-permute-start.2 = (bf16[128,1024]{1,0:T(8,128)(2,1)}, bf16[128,1024]{1,0:T(8,128)(2,1)S(1)}, u32[]{:S(2)}, u32[]{:S(2)}) collective-permute-start(bf16[128,1024]{1,0:T(8,128)(2,1)} %param.5), channel_id=1, source_target_pairs={{0,3},{1,0},{2,1},{3,2},{4,7},{5,4},{6,5},{7,6},{8,11},{9,8},{10,9... | collective-permute-start | bytes 786440 | tf_op jit(solution)/shard_map/ppermute | solution.py:35
  9.8 13.1 %collective-permute-start.1 = (bf16[128,1024]{1,0:T(8,128)(2,1)}, bf16[128,1024]{1,0:T(8,128)(2,1)S(1)}, u32[]{:S(2)}, u32[]{:S(2)}) collective-permute-start(bf16[128,1024]{1,0:T(8,128)(2,1)} %param.5), channel_id=1, source_target_pairs={{0,2},{1,3},{2,0},{3,1},{4,6},{5,7},{6,4},{7,5},{8,10},{9,11},{10,... | collective-permute-start | bytes 786440 | tf_op jit(solution)/shard_map/ppermute | solution.py:35
  25.8 1.9 copy-start.5
  25.8 2.4 %copy-start.4 = (bf16[1024,1024]{1,0:T(8,128)(2,1)S(1)}, bf16[1024,1024]{1,0:T(8,128)(2,1)}, u32[]{:S(2)}) copy-start(bf16[1024,1024]{1,0:T(8,128)(2,1)} %copy.52) | copy-start | bytes 6291460
  40.2 3.8 %collective-permute-start.3 = (f32[2,1536,128]{1,2,0:T(8,128)}, f32[2,1536,128]{1,2,0:T(8,128)}, u32[]{:S(2)}, u32[]{:S(2)}) collective-permute-start(f32[2,1536,128]{1,2,0:T(8,128)} %bitcast.152), channel_id=1, source_target_pairs={{0,4},{4,0},{8,12},{12,8},{1,5},{5,1},{9,13},{13,9},{2,6},{6,2},{1... | collective-permute-start | bytes 4718600 | tf_op jit(solution)/shard_map/ppermute | solution.py:30
  46.0 1.2 copy-start.2
  47.2 22.2 %collective-permute-start.4 = (bf16[1536,128]{0,1:T(8,128)(2,1)S(1)}, bf16[1536,128]{0,1:T(8,128)(2,1)S(1)}, u32[]{:S(2)}, u32[]{:S(2)}) collective-permute-start(bf16[1536,128]{0,1:T(8,128)(2,1)S(1)} %fusion.61), channel_id=1, source_target_pairs={{0,8},{4,12},{8,0},{12,4},{1,9},{5,13},{9,1},{13,5},{2,10},{6,14},... | collective-permute-start | bytes 1179656 | tf_op jit(solution)/shard_map/ppermute | solution.py:30
  70.7 0.6 copy-start.6
  77.8 7.7 %copy-start.3 = (f32[512,256]{1,0:T(8,128)S(1)}, f32[512,256]{1,0:T(8,128)}, u32[]{:S(2)}) copy-start(f32[512,256]{1,0:T(8,128)} %reshape_reshape.5) | copy-start | bytes 1572868
  87.3 1.9 collective-permute-start.5
  157.5 2.3 copy-start.8
  159.9 2.3 copy-start.9
  164.5 2.5 %copy-start.1 = (f32[4,512,256]{1,2,0:T(8,128)S(1)}, f32[4,512,256]{1,2,0:T(8,128)}, u32[]{:S(2)}) copy-start(f32[4,512,256]{1,2,0:T(8,128)} %get-tuple-element.51) | copy-start | bytes 6291460
  189.4 2.0 collective-permute-start.7
  189.5 1.9 collective-permute-start.8
  190.1 1.3 collective-permute-start.6
  191.7 1.6 collective-permute-start.9
  194.2 14.4 %collective-permute-start.10 = (bf16[2,512,256]{2,1,0:T(8,128)(2,1)}, bf16[2,512,256]{2,1,0:T(8,128)(2,1)S(1)}, u32[]{:S(2)}, u32[]{:S(2)}) collective-permute-start(bf16[2,512,256]{2,1,0:T(8,128)(2,1)} %pad_maximum_fusion.2), channel_id=1, source_target_pairs={{0,8},{4,12},{8,0},{12,4},{1,9},{5,13},{9,1},{13,5},{2,10},{6,14},... | collective-permute-start | bytes 1572872 | tf_op jit(solution)/shard_map/ppermute | solution.py:30
  210.8 9.7 %collective-permute-start.11 = (bf16[128,1024]{1,0:T(8,128)(2,1)}, bf16[128,1024]{1,0:T(8,128)(2,1)}, u32[]{:S(2)}, u32[]{:S(2)}) collective-permute-start(bf16[128,1024]{1,0:T(8,128)(2,1)} %get-tuple-element.19), channel_id=1, source_target_pairs={{0,1},{1,2},{2,3},{3,0},{4,5},{5,6},{6,7},{7,4},{8,9},{9,10},{10,1... | collective-permute-start | bytes 786440 | tf_op jit(solution)/shard_map/ppermute | solution.py:35
  212.3 12.4 %collective-permute-start.13 = (bf16[128,1024]{1,0:T(8,128)(2,1)}, bf16[128,1024]{1,0:T(8,128)(2,1)}, u32[]{:S(2)}, u32[]{:S(2)}) collective-permute-start(bf16[128,1024]{1,0:T(8,128)(2,1)} %get-tuple-element.20), channel_id=1, source_target_pairs={{0,3},{1,0},{2,1},{3,2},{4,7},{5,4},{6,5},{7,6},{8,11},{9,8},{10,9... | collective-permute-start | bytes 786440 | tf_op jit(solution)/shard_map/ppermute | solution.py:35
  214.0 12.4 %collective-permute-start.12 = (bf16[128,1024]{1,0:T(8,128)(2,1)S(1)}, bf16[128,1024]{1,0:T(8,128)(2,1)}, u32[]{:S(2)}, u32[]{:S(2)}) collective-permute-start(bf16[128,1024]{1,0:T(8,128)(2,1)S(1)} %get-tuple-element.21), channel_id=1, source_target_pairs={{0,2},{1,3},{2,0},{3,1},{4,6},{5,7},{6,4},{7,5},{8,10},{9,11},{10,... | collective-permute-start | bytes 786440 | tf_op jit(solution)/shard_map/ppermute | solution.py:35
Sparse Core Ops, SparseCore 0:
  72.2 85.3 all-gather.2
where the time goes:
time: 238 us; the launch traced here: 236 us
  waiting for transfers between devices  102 us (43%)
  local copies, waits for them, and re-layouts  37 us (16%)
  matrix products  31.4 us (13%)
  other arithmetic  26 us (11%)
  starting transfers between devices  24.5 us (10%)
  between operations  14.3 us (6%)
    all_gather x1, waiting for transfers between devices, on_device(): kv_all = lax.all_gather(kv_own, 'seq', axis=0, tiled=False)  62.2 us
    ppermute x8, waiting for transfers between devices, swap_pairs(): return lax.ppermute(value, 'row', [(r, r ^ flip) for r in range(count)])  26.8 us
    ppermute x8, starting transfers between devices, swap_pairs(): return lax.ppermute(value, 'row', [(r, r ^ flip) for r in range(count)])  14.2 us
    ppermute x6, waiting for transfers between devices, shifted(): lax.ppermute(value, axis, [(i, (i + step) % count) for i in range(count)])  13.4 us
    dot_general x5, matrix products, attend(): jnp.einsum('hqk,kd->hqd', weights.astype(jnp.bfloat16), value_blk, prefer...  13.2 us
    dot_general x5, matrix products, attend(): jnp.einsum('hqd,kd->hqk', q_heads, key_blk, preferred_element_type=jnp.fl...  12.1 us
    ppermute x6, starting transfers between devices, shifted(): lax.ppermute(value, axis, [(i, (i + step) % count) for i in range(count)])  10.3 us
    reduce_sum x5, other arithmetic, attend(): total = total * factor + jnp.sum(weights, axis=-1)  8.97 us
  transfers between devices with their start and end apart: 15, of which 12 were waited for; matrix products, arithmetic and copies ran while one was open for 15% of the time, Pallas kernels for 0%

commit v1 on v0

--- a/solution.py
+++ b/solution.py
@@ -122,15 +122,23 @@
         jnp.zeros((n_heads, block_len), jnp.float32),
         jnp.zeros((n_heads, block_len, HEAD_DIM), jnp.float32),
     )
-    kv_all = lax.all_gather(kv_own, "seq", axis=0, tiled=False)
+    parts = 1
+    part_len = key_len // parts
+    kv_parts = kv_own.reshape(parts, part_len, -1)
+    gathered = [
+        lax.all_gather(kv_parts[p].reshape(-1), "seq", axis=0, tiled=True).reshape(seq_count, part_len, -1)
+        for p in range(parts)
+    ]
     own_pos = block_start + k_offset
     state = attend(state, kv_own, own_pos[None, :] <= q_pos[:, None])
-    per_chunk = 4
-    for first in range(0, seq_count, per_chunk):
-        kv_chunk = kv_all[first : first + per_chunk].reshape(per_chunk * key_len, -1)
-        blocks = first + jnp.arange(per_chunk, dtype=jnp.int32)
-        chunk_pos = (blocks[:, None] * block_len + k_offset[None, :]).reshape(-1)
-        state = attend(state, kv_chunk, (chunk_pos < block_start)[None, :])
+    per_chunk = seq_count // 2
+    for p in range(parts):
+        for first in range(0, seq_count, per_chunk):
+            kv_chunk = gathered[p][first : first + per_chunk].reshape(per_chunk * part_len, -1)
+            blocks = first + jnp.arange(per_chunk, dtype=jnp.int32)
+            part_offset = core * key_len + p * part_len + jnp.arange(part_len, dtype=jnp.int32)
+            chunk_pos = (blocks[:, None] * block_len + part_offset[None, :]).reshape(-1)
+            state = attend(state, kv_chunk, (chunk_pos < block_start)[None, :])
 
     peak, total, summed = state
     own = n_heads // 2

time: 238 us -> 242 us (1.017)
  starting transfers between devices: 24.5 us -> 12.4 us
  waiting for transfers between devices: 102 us -> 110 us
  local copies, waits for them, and re-layouts: 37 us -> 42.3 us
  other arithmetic: 26 us -> 30.1 us
    ppermute x8, starting transfers between devices: 14.2 us -> 3.27 us  [swap_pairs(): return lax.ppermute(value, 'row', [(r, r ^ flip) for r in range(count)])]
    slice x0 -> x3, local copies, waits for them, and re-layouts: none -> 7.41 us  [on_device(): gathered[p][first:first + per_chunk].reshape(per_chunk * part_len, -1)]
    ppermute x6, waiting for transfers between devices: 13.4 us -> 20.4 us  [shifted(): lax.ppermute(value, axis, [(i, (i + step) % count) for i in range(count)])]
    reduce_sum x5 -> x3, other arithmetic: 8.97 us -> 12.3 us  [attend(): total = total * factor + jnp.sum(weights, axis=-1)]
    dot_general x5 -> x3, matrix products: 12.1 us -> 13.8 us  [attend(): jnp.einsum('hqd,kd->hqk', q_heads, key_blk, preferred_element_type=jnp.fl...]
    dot_general x5 -> x3, matrix products: 13.2 us -> 12.2 us  [attend(): jnp.einsum('hqk,kd->hqd', weights.astype(jnp.bfloat16), value_blk, prefer...]
  transfers between devices with their start and end apart: 15 -> 15, of which waited for: 12 -> 11; matrix products, arithmetic and copies ran while one was open for 15% -> 13% of each run, Pallas kernels for 0% -> 0%
where the time goes in v1:
time: 242 us; the launch traced here: 239 us
  waiting for transfers between devices  110 us (45%)
  local copies, waits for them, and re-layouts  42.3 us (17%)
  matrix products  30.8 us (13%)
  other arithmetic  30.1 us (12%)
  between operations  13.8 us (6%)
  starting transfers between devices  12.4 us (5%)
    all_gather x1, waiting for transfers between devices, on_device(): lax.all_gather(kv_parts[p].reshape(-1), 'seq', axis=0, tiled=True)  61.6 us
    ppermute x8, waiting for transfers between devices, swap_pairs(): return lax.ppermute(value, 'row', [(r, r ^ flip) for r in range(count)])  28 us
    ppermute x6, waiting for transfers between devices, shifted(): lax.ppermute(value, axis, [(i, (i + step) % count) for i in range(count)])  20.4 us
    dot_general x3, matrix products, attend(): jnp.einsum('hqd,kd->hqk', q_heads, key_blk, preferred_element_type=jnp.fl...  13.8 us
    reduce_sum x3, other arithmetic, attend(): total = total * factor + jnp.sum(weights, axis=-1)  12.3 us
    dot_general x3, matrix products, attend(): jnp.einsum('hqk,kd->hqd', weights.astype(jnp.bfloat16), value_blk, prefer...  12.2 us
    ppermute x6, starting transfers between devices, shifted(): lax.ppermute(value, axis, [(i, (i + step) % count) for i in range(count)])  9.12 us
    slice x3, local copies, waits for them, and re-layouts, on_device(): gathered[p][first:first + per_chunk].reshape(per_chunk * part_len, -1)  7.41 us
  transfers between devices with their start and end apart: 15, of which 11 were waited for; matrix products, arithmetic and copies ran while one was open for 13% of the time, Pallas kernels for 0%

profile of v1, /device:TPU:2, one launch (start us, length us, event | category | flops | bytes accessed | tf_op | source)
XLA Modules:
  0.0 239.5 jit_solution(14542524109298533965)
XLA Ops:
  6.5 3.1 %collective-permute-start.2 = (bf16[128,1024]{1,0:T(8,128)(2,1)}, bf16[128,1024]{1,0:T(8,128)(2,1)}, u32[]{:S(2)}, u32[]{:S(2)}) collective-permute-start(bf16[128,1024]{1,0:T(8,128)(2,1)} %param.5), channel_id=1, source_target_pairs={{0,3},{1,0},{2,1},{3,2},{4,7},{5,4},{6,5},{7,6},{8,11},{9,8},{10,9... | collective-permute-start | bytes 786440 | tf_op jit(solution)/shard_map/ppermute | solution.py:35
  9.6 0.6 collective-permute-start.1
  10.3 1.0 collective-permute-start
  11.4 4.0 %copy.68 = bf16[1024,1024]{1,0:T(8,128)(2,1)} copy(bf16[1024,1024]{0,1:T(8,128)(2,1)} %bitcast.124) | data formatting | bytes 4194304 | tf_op jit(solution)/shard_map/dot_general | solution.py:64
  15.4 1.0 copy.69
  16.4 1.0 copy.70
  17.4 3.7 %collective-permute-done.2 = bf16[128,1024]{1,0:T(8,128)(2,1)} collective-permute-done((bf16[128,1024]{1,0:T(8,128)(2,1)}, bf16[128,1024]{1,0:T(8,128)(2,1)}, u32[]{:S(2)}, u32[]{:S(2)}) %collective-permute-start.2) | collective-permute-done | bytes 262176 | tf_op jit(solution)/shard_map/ppermute | solution.py:35
  21.1 3.7 %collective-permute-done = bf16[128,1024]{1,0:T(8,128)(2,1)} collective-permute-done((bf16[128,1024]{1,0:T(8,128)(2,1)}, bf16[128,1024]{1,0:T(8,128)(2,1)}, u32[]{:S(2)}, u32[]{:S(2)}) %collective-permute-start) | collective-permute-done | bytes 262176 | tf_op jit(solution)/shard_map/ppermute | solution.py:35
  24.8 1.2 pad_maximum_fusion
  26.1 1.6 gather_fusion
  27.7 1.6 broadcast_select_fusion.1
  29.6 2.6 %convolution_bitcast_fusion = f32[4,512,256]{2,1,0:T(8,128)} fusion(bf16[512,1024,1]{1,0,2:T(8,128)(2,1)S(1)} %bitcast.134, bf16[4,256,1024]{2,1,0:T(8,128)(2,1)S(1)} %bitcast.125), kind=kOutput, calls=%fused_computation.19 | convolution fusion | flops 1073741824 | bytes 5242880 | tf_op jit(solution)/shard_map/dot_general | solution.py:64
  32.2 2.6 %reshape.341 = f32[2,2,1024,128]{3,2,1,0:T(8,128)} reshape(f32[4,512,256]{2,1,0:T(8,128)} %convolution_bitcast_fusion) | data formatting | bytes 4194304 | tf_op jit(solution)/shard_map/reshape | solution.py:68
  34.9 1.8 constant_dynamic-update-slice_fusion
  37.8 1.9 constant_dynamic-slice_fusion.1
  39.7 3.0 %copy.48 = f32[2,1,1536,128]{2,3,0,1:T(8,128)} copy(f32[2,1,1536,128]{3,2,1,0:T(8,128)} %get-tuple-element.14) | data formatting | bytes 3145728 | tf_op jit(solution)/shard_map/jit(dynamic_index_in_dim)/dynamic_slice | solution.py:76
  42.7 3.1 %copy.47 = f32[2,1,1536,128]{2,3,0,1:T(8,128)} copy(f32[2,1,1536,128]{3,2,1,0:T(8,128)} %get-tuple-element.13) | data formatting | bytes 3145728 | tf_op jit(solution)/shard_map/jit(dynamic_index_in_dim)/dynamic_slice | solution.py:75
  45.8 0.7 collective-permute-done.3
  46.5 2.1 bitcast_add_fusion
  48.6 1.2 copy-done.2
  49.8 0.8 collective-permute-start.4
  50.9 10.3 %collective-permute-done.4 = bf16[1536,128]{0,1:T(8,128)(2,1)S(1)} collective-permute-done((bf16[1536,128]{0,1:T(8,128)(2,1)S(1)}, bf16[1536,128]{0,1:T(8,128)(2,1)S(1)}, u32[]{:S(2)}, u32[]{:S(2)}) %collective-permute-start.4) | collective-permute-done | bytes 393248 | tf_op jit(solution)/shard_map/ppermute | solution.py:30
  61.2 1.2 bitcast_add_fusion.1
  62.5 0.6 copy-done.9
  63.2 0.8 copy.75
  64.1 1.0 multiply_cosine_fusion
  65.0 1.0 pad_maximum_fusion.3
  66.1 0.8 slice.104
  67.0 1.2 copy.49
  68.2 1.0 reshape_reshape.5
  69.8 2.4 %maximum_multiply_fusion = f32[512,2,128]{2,1,0:T(2,128)} fusion(f32[512,2,64]{2,1,0:T(2,128)S(1)} %get-tuple-element.27, f32[512,2,64]{2,1,0:T(2,128)S(1)} %get-tuple-element.26, f32[512,128]{1,0:T(8,128)} %get-tuple-element.49), kind=kLoop, calls=%fused_computation.55 | loop fusion | flops 262144 | bytes 1310720 | tf_op jit(solution)/shard_map/mul | solution.py:24
  72.2 2.1 copy.51
  74.3 2.0 copy.52
  76.3 1.1 mul.158
  77.5 1.8 fusion.28
  79.5 1.7 collective-permute-done.5
  81.2 1.1 pad_maximum_fusion.1
  82.2 1.0 copy.53
  83.3 1.3 copy.54
  84.6 2.8 %fusion.12 = (f32[4,512]{1,0:T(4,128)S(1)}, f32[4,512,256]{1,2,0:T(8,128)}) fusion(pred[512,256]{0,1:T(8,128)(4,1)S(1)} %broadcast_compare_fusion, bf16[256,128]{0,1:T(8,128)(2,1)} %copy-done.9, bf16[512,4,128]{2,0,1:T(8,128)(2,1)S(1)} %copy.54), kind=kOutput, calls=%fused_computation.18 | convolution fusion | flops 135788544 | bytes 2826240 | tf_op jit(solution)/shard_map/hqd,kd->hqk/dot_general | solution.py:104
  87.3 61.6 %all-gather.2.cloned.1.call-done = bf16[1048576]{0:T(1024)(128)(2,1)} async-done(((bf16[65536]{0:T(1024)(128)(2,1)}), bf16[1048576]{0:T(1024)(128)(2,1)}) %all-gather.2.cloned.1.call-update) | async-done | bytes 2097168 | tf_op jit(solution)/shard_map/all_gather | solution.py:129
  149.0 3.0 %fusion.68 = (bf16[524288]{0:T(1024)(128)(2,1)}, bf16[524288]{0:T(1024)(128)(2,1)}) fusion(bf16[1048576]{0:T(1024)(128)(2,1)} %all-gather.2.cloned.1.call-done), kind=kLoop, calls=%fused_computation.148 | loop fusion | bytes 4194304 | tf_op jit(solution)/shard_map/slice | solution.py:137
  152.0 2.2 slice.93
  154.2 2.2 slice.89
  156.4 8.3 %fusion.1 = (f32[4,512]{1,0:T(4,128)S(1)}, f32[4,512,2048]{2,1,0:T(8,128)}) fusion(pred[2048]{0:T(1024)(128)(4,1)S(1)} %lt.112, bf16[2048,256]{1,0:T(8,128)(2,1)} %slice.93, bf16[512,4,128]{2,0,1:T(8,128)(2,1)S(1)} %copy.54), kind=kOutput, calls=%fused_computation.6 | convolution fusion | flops 1086322688 | bytes 17836032 | tf_op jit(solution)/shard_map/hqd,kd->hqk/dot_general | solution.py:104
  164.7 2.7 %fusion = (f32[4,512]{1,0:T(4,128)S(1)}, f32[4,512,2048]{2,1,0:T(8,128)S(1)}) fusion(pred[2048]{0:T(1024)(128)(4,1)S(1)} %lt.110, bf16[2048,256]{1,0:T(8,128)(2,1)S(1)} %copy-done.3, bf16[512,4,128]{2,0,1:T(8,128)(2,1)S(1)} %copy.54), kind=kOutput, calls=%fused_computation.5 | convolution fusion | flops 1086322688 | bytes 17836032 | tf_op jit(solution)/shard_map/hqd,kd->hqk/dot_general | solution.py:104
  167.5 7.7 %fusion.6 = f32[4,512,128]{1,2,0:T(8,128)S(1)} fusion(f32[4,512,2048]{2,1,0:T(8,128)} %get-tuple-element.39, f32[4,512]{1,0:T(4,128)S(1)} %get-tuple-element.11, pred[2048]{0:T(1024)(128)(4,1)S(1)} %lt.112, bf16[2048,256]{1,0:T(8,128)(2,1)S(1)} %copy-done.4), kind=kOutput, calls=%fused_computation.11 | convolution fusion | flops 1090519040 | bytes 18360320 | tf_op jit(solution)/shard_map/hqk,kd->hqd/dot_general | solution.py:112
  175.1 7.8 %fusion.4 = f32[4,512]{1,0:T(4,128)S(1)} fusion(f32[4,512,2048]{2,1,0:T(8,128)} %get-tuple-element.39, f32[4,512]{1,0:T(4,128)S(1)} %get-tuple-element.11, pred[2048]{0:T(1024)(128)(4,1)S(1)} %lt.112), kind=kLoop, calls=%fused_computation.9 | loop fusion | flops 16775168 | bytes 16795648 | tf_op jit(solution)/shard_map/reduce_sum | solution.py:111
  182.9 3.7 %fusion.8 = f32[4,512,128]{1,2,0:T(8,128)S(1)} fusion(f32[4,512,2048]{2,1,0:T(8,128)S(1)} %get-tuple-element.41, f32[4,512]{1,0:T(4,128)S(1)} %get-tuple-element.12, pred[2048]{0:T(1024)(128)(4,1)S(1)} %lt.110, bf16[2048,256]{1,0:T(8,128)(2,1)S(1)} %copy-done.3), kind=kOutput, calls=%fused_computation.12 | convolution fusion | flops 1090519040 | bytes 18360320 | tf_op jit(solution)/shard_map/hqk,kd->hqd/dot_general | solution.py:112
  186.6 4.0 %fusion.2 = f32[4,512]{1,0:T(4,128)S(1)} fusion(f32[4,512,2048]{2,1,0:T(8,128)S(1)} %get-tuple-element.41, f32[4,512]{1,0:T(4,128)S(1)} %get-tuple-element.12, pred[2048]{0:T(1024)(128)(4,1)S(1)} %lt.110), kind=kLoop, calls=%fused_computation.7 | loop fusion | flops 16775168 | bytes 16795648 | tf_op jit(solution)/shard_map/reduce_sum | solution.py:111
  191.2 0.8 fusion.18
  192.8 1.2 collective-permute-done.8
  194.6 1.4 collective-permute-done.9
  196.0 0.9 pad_maximum_fusion.2
  196.9 1.5 collective-permute-start.10
  198.3 12.7 %collective-permute-done.10 = bf16[2,512,256]{2,1,0:T(8,128)(2,1)S(1)} collective-permute-done((bf16[2,512,256]{2,1,0:T(8,128)(2,1)}, bf16[2,512,256]{2,1,0:T(8,128)(2,1)S(1)}, u32[]{:S(2)}, u32[]{:S(2)}) %collective-permute-start.10) | collective-permute-done | bytes 524320 | tf_op jit(solution)/shard_map/ppermute | solution.py:30
  211.1 1.3 bitcast_convert_fusion
  212.4 0.8 dynamic-slice_bitcast_fusion.2
  213.2 2.7 %collective-permute-start.13 = (bf16[128,1024]{1,0:T(8,128)(2,1)}, bf16[128,1024]{1,0:T(8,128)(2,1)}, u32[]{:S(2)}, u32[]{:S(2)}) collective-permute-start(bf16[128,1024]{1,0:T(8,128)(2,1)} %get-tuple-element.18), channel_id=1, source_target_pairs={{0,3},{1,0},{2,1},{3,2},{4,7},{5,4},{6,5},{7,6},{8,11},{9,8},{10,9... | collective-permute-start | bytes 786440 | tf_op jit(solution)/shard_map/ppermute | solution.py:35
  216.0 0.8 collective-permute-start.12
  216.8 0.9 collective-permute-start.11
  217.7 9.3 %collective-permute-done.13 = bf16[128,1024]{1,0:T(8,128)(2,1)} collective-permute-done((bf16[128,1024]{1,0:T(8,128)(2,1)}, bf16[128,1024]{1,0:T(8,128)(2,1)}, u32[]{:S(2)}, u32[]{:S(2)}) %collective-permute-start.13) | collective-permute-done | bytes 262176 | tf_op jit(solution)/shard_map/ppermute | solution.py:35
  227.0 3.6 %collective-permute-done.11 = bf16[128,1024]{1,0:T(8,128)(2,1)} collective-permute-done((bf16[128,1024]{1,0:T(8,128)(2,1)S(1)}, bf16[128,1024]{1,0:T(8,128)(2,1)}, u32[]{:S(2)}, u32[]{:S(2)}) %collective-permute-start.11) | collective-permute-done | bytes 262176 | tf_op jit(solution)/shard_map/ppermute | solution.py:35
  230.6 2.0 fusion.35
  (76 shorter events, 4.9 us)
Async XLA Ops:
  6.5 204.6 %copy-start = (bf16[1024,1024]{1,0:T(8,128)(2,1)S(1)}, bf16[1024,1024]{1,0:T(8,128)(2,1)}, u32[]{:S(2)}) copy-start(bf16[1024,1024]{1,0:T(8,128)(2,1)} %param.9) | copy-start | bytes 6291460
  6.5 8.8 %copy-start.10 = (bf16[1024,256]{1,0:T(8,128)(2,1)S(1)}, bf16[1024,256]{1,0:T(8,128)(2,1)}, u32[]{:S(2)}) copy-start(bf16[1024,256]{1,0:T(8,128)(2,1)} %param.7) | copy-start | bytes 1572868
  6.5 9.9 %copy-start.11 = (bf16[1024,256]{1,0:T(8,128)(2,1)S(1)}, bf16[1024,256]{1,0:T(8,128)(2,1)}, u32[]{:S(2)}) copy-start(bf16[1024,256]{1,0:T(8,128)(2,1)} %param.8) | copy-start | bytes 1572868
  6.5 142.4 %all-gather.2.cloned.1.call-start = ((), (), s32[]{:S(2)}) async-start(), calls=%async_computation | async-start | bytes 2228224 | tf_op jit(solution)/shard_map/all_gather | solution.py:129
  6.5 14.6 %collective-permute-start.2 = (bf16[128,1024]{1,0:T(8,128)(2,1)}, bf16[128,1024]{1,0:T(8,128)(2,1)}, u32[]{:S(2)}, u32[]{:S(2)}) collective-permute-start(bf16[128,1024]{1,0:T(8,128)(2,1)} %param.5), channel_id=1, source_target_pairs={{0,3},{1,0},{2,1},{3,2},{4,7},{5,4},{6,5},{7,6},{8,11},{9,8},{10,9... | collective-permute-start | bytes 786440 | tf_op jit(solution)/shard_map/ppermute | solution.py:35
  9.6 11.5 %collective-permute-start.1 = (bf16[128,1024]{1,0:T(8,128)(2,1)}, bf16[128,1024]{1,0:T(8,128)(2,1)}, u32[]{:S(2)}, u32[]{:S(2)}) collective-permute-start(bf16[128,1024]{1,0:T(8,128)(2,1)} %param.5), channel_id=1, source_target_pairs={{0,2},{1,3},{2,0},{3,1},{4,6},{5,7},{6,4},{7,5},{8,10},{9,11},{10,... | collective-permute-start | bytes 786440 | tf_op jit(solution)/shard_map/ppermute | solution.py:35
  10.3 14.6 %collective-permute-start = (bf16[128,1024]{1,0:T(8,128)(2,1)}, bf16[128,1024]{1,0:T(8,128)(2,1)}, u32[]{:S(2)}, u32[]{:S(2)}) collective-permute-start(bf16[128,1024]{1,0:T(8,128)(2,1)} %param.5), channel_id=1, source_target_pairs={{0,1},{1,2},{2,3},{3,0},{4,5},{5,6},{6,7},{7,4},{8,9},{9,10},{10,1... | collective-permute-start | bytes 786440 | tf_op jit(solution)/shard_map/ppermute | solution.py:35
  11.4 13.5 %copy-start.12 = (bf16[128,1024]{1,0:T(8,128)(2,1)S(1)}, bf16[128,1024]{1,0:T(8,128)(2,1)}, u32[]{:S(2)}) copy-start(bf16[128,1024]{1,0:T(8,128)(2,1)} %param.5) | copy-start | bytes 786436
  27.7 1.9 copy-start.6
  34.9 1.8 copy-start.8
  34.9 2.3 copy-start.7
  42.7 3.8 %collective-permute-start.3 = (f32[2,1536,128]{1,2,0:T(8,128)}, f32[2,1536,128]{1,2,0:T(8,128)}, u32[]{:S(2)}, u32[]{:S(2)}) collective-permute-start(f32[2,1536,128]{1,2,0:T(8,128)} %bitcast.130), channel_id=1, source_target_pairs={{0,4},{4,0},{8,12},{12,8},{1,5},{5,1},{9,13},{13,9},{2,6},{6,2},{1... | collective-permute-start | bytes 4718600 | tf_op jit(solution)/shard_map/ppermute | solution.py:30
  48.5 1.2 copy-start.2
  49.8 11.4 %collective-permute-start.4 = (bf16[1536,128]{0,1:T(8,128)(2,1)S(1)}, bf16[1536,128]{0,1:T(8,128)(2,1)S(1)}, u32[]{:S(2)}, u32[]{:S(2)}) collective-permute-start(bf16[1536,128]{0,1:T(8,128)(2,1)S(1)} %fusion.41), channel_id=1, source_target_pairs={{0,8},{4,12},{8,0},{12,4},{1,9},{5,13},{9,1},{13,5},{2,10},{6,14},... | collective-permute-start | bytes 1179656 | tf_op jit(solution)/shard_map/ppermute | solution.py:30
  62.5 0.6 copy-start.9
  69.8 7.7 %copy-start.5 = (f32[512,256]{1,0:T(8,128)S(1)}, f32[512,256]{1,0:T(8,128)}, u32[]{:S(2)}) copy-start(f32[512,256]{1,0:T(8,128)} %reshape_reshape.5) | copy-start | bytes 1572868
  79.3 1.9 collective-permute-start.5
  156.4 8.3 %copy-start.3 = (bf16[2048,256]{1,0:T(8,128)(2,1)S(1)}, bf16[2048,256]{1,0:T(8,128)(2,1)}, u32[]{:S(2)}) copy-start(bf16[2048,256]{1,0:T(8,128)(2,1)} %slice.89) | copy-start | bytes 3145732
  164.7 2.8 %copy-start.4 = (bf16[2048,256]{1,0:T(8,128)(2,1)S(1)}, bf16[2048,256]{1,0:T(8,128)(2,1)}, u32[]{:S(2)}) copy-start(bf16[2048,256]{1,0:T(8,128)(2,1)} %slice.93) | copy-start | bytes 3145732
  186.6 4.0 %copy-start.1 = (f32[4,512,256]{1,2,0:T(8,128)S(1)}, f32[4,512,256]{1,2,0:T(8,128)}, u32[]{:S(2)}) copy-start(f32[4,512,256]{1,2,0:T(8,128)} %get-tuple-element.43) | copy-start | bytes 6291460
  192.0 2.0 collective-permute-start.7
  192.1 1.9 collective-permute-start.8
  192.7 1.3 collective-permute-start.6
  194.3 1.6 collective-permute-start.9
  196.9 14.2 %collective-permute-start.10 = (bf16[2,512,256]{2,1,0:T(8,128)(2,1)}, bf16[2,512,256]{2,1,0:T(8,128)(2,1)S(1)}, u32[]{:S(2)}, u32[]{:S(2)}) collective-permute-start(bf16[2,512,256]{2,1,0:T(8,128)(2,1)} %pad_maximum_fusion.2), channel_id=1, source_target_pairs={{0,8},{4,12},{8,0},{12,4},{1,9},{5,13},{9,1},{13,5},{2,10},{6,14},... | collective-permute-start | bytes 1572872 | tf_op jit(solution)/shard_map/ppermute | solution.py:30
  213.2 13.7 %collective-permute-start.13 = (bf16[128,1024]{1,0:T(8,128)(2,1)}, bf16[128,1024]{1,0:T(8,128)(2,1)}, u32[]{:S(2)}, u32[]{:S(2)}) collective-permute-start(bf16[128,1024]{1,0:T(8,128)(2,1)} %get-tuple-element.18), channel_id=1, source_target_pairs={{0,3},{1,0},{2,1},{3,2},{4,7},{5,4},{6,5},{7,6},{8,11},{9,8},{10,9... | collective-permute-start | bytes 786440 | tf_op jit(solution)/shard_map/ppermute | solution.py:35
  216.0 11.0 %collective-permute-start.12 = (bf16[128,1024]{1,0:T(8,128)(2,1)}, bf16[128,1024]{1,0:T(8,128)(2,1)}, u32[]{:S(2)}, u32[]{:S(2)}) collective-permute-start(bf16[128,1024]{1,0:T(8,128)(2,1)} %get-tuple-element.19), channel_id=1, source_target_pairs={{0,2},{1,3},{2,0},{3,1},{4,6},{5,7},{6,4},{7,5},{8,10},{9,11},{10,... | collective-permute-start | bytes 786440 | tf_op jit(solution)/shard_map/ppermute | solution.py:35
  216.8 13.8 %collective-permute-start.11 = (bf16[128,1024]{1,0:T(8,128)(2,1)S(1)}, bf16[128,1024]{1,0:T(8,128)(2,1)}, u32[]{:S(2)}, u32[]{:S(2)}) collective-permute-start(bf16[128,1024]{1,0:T(8,128)(2,1)S(1)} %get-tuple-element.17), channel_id=1, source_target_pairs={{0,1},{1,2},{2,3},{3,0},{4,5},{5,6},{6,7},{7,4},{8,9},{9,10},{10,1... | collective-permute-start | bytes 786440 | tf_op jit(solution)/shard_map/ppermute | solution.py:35
Sparse Core Ops, SparseCore 0:
  64.1 84.7 all-gather.1
